TPU v7x, 256 devices: a whole 4x4x8 slice. The times are simulated.
256 devices in a mesh: gx: 8 (over x, core), gy: 32 (over y, z).
Axes of the slice: x: 4, y: 4, z: 8, core: 2. Of those that a mesh axis runs over, the one named last changes fastest.
Arguments:
- cells: bfloat16 [256, 1048576], P(None, ('gx', 'gy')), may hold values from -25 to 25
- send_index: int32 [8192, 2], P(('gx', 'gy')), may hold values from 0 to 31
- send_count: int32 [8192], P(('gx', 'gy')), may hold values from 1 to 2, as said below
- prolong_block: int32 [8192, 4], P(('gx', 'gy')), may hold values from 0 to 63, as said below
- prolong_level: int32 [8192, 4], P(('gx', 'gy')), may hold values from 0 to 3
- prolong_maps: bfloat16 [4, 128, 512], replicated, may hold values from -0.25 to 0.25
Outputs:
- factor: float32 [256, 256], replicated
- modes: float32 [128, 4194304], P(None, ('gx', 'gy'))
Inputs may be any that keep to these rules, and one draw needn't show every extreme that they name: `send_count`: every sender and owner pair uses 1 to 2 slots; some pair uses all 2. `prolong_block`: the first slot feeding each brick is slot 0 of some sender, a multiple of 2.
All inputs are finite; a program needn't handle non-finite values.
Results may differ from a plain program's by a relative error of at most 0.0041.
Values may be sent and summed in bfloat16 or wider, within the bound.
No kernel may reach another device: no remote copies, remote signals or barrier semaphores. Data moves between devices by JAX's collectives and lax.ppermute only.
A program may use at most 128 MiB of HBM per device.

v0:
```python
import jax
import jax.numpy as jnp
from jax import lax
from jax.sharding import PartitionSpec as P

RANK = 128
BLK = 128


def from_partner(value, axis, bit):
    mask = 2**bit
    pairs = [(source, source ^ mask) for source in range(lax.axis_size(axis))]
    return lax.ppermute(value, axis, pairs)


def lift(received, blocks, levels, maps):
    picked = jnp.take(received, blocks, axis=1)
    chosen = jnp.take(maps, levels, axis=0)
    lifted = jnp.einsum("sbnc,bncd->sbd", picked, chosen, preferred_element_type=jnp.float32)
    return lifted.reshape(lifted.shape[0], -1).astype(jnp.bfloat16)


def combined(factor, other):
    mine = jnp.dot(factor, factor.T, precision=lax.Precision.HIGHEST)
    theirs = jnp.dot(other, other.T, precision=lax.Precision.HIGHEST)
    return jnp.linalg.cholesky(mine + theirs)


def body(cells, send_index, send_count, prolong_block, prolong_level, prolong_maps):
    snaps = cells.shape[0]
    local = cells.reshape(snaps, -1, BLK)
    peers, slots = send_index.shape
    outgoing = jnp.take(local, send_index.reshape(-1), axis=1)
    live = (jnp.arange(slots, dtype=jnp.int32)[None, :] < send_count[:, None]).reshape(-1)
    outgoing = outgoing * live[None, :, None].astype(jnp.bfloat16)
    received = lax.all_to_all(outgoing, "gy", split_axis=1, concat_axis=1, tiled=True)
    bricks = lift(received, prolong_block, prolong_level, prolong_maps)
    gram = lax.dot_general(
        bricks, bricks, (((1,), (1,)), ((), ())), preferred_element_type=jnp.float32
    )
    total_cells = lax.axis_size("gx") * lax.axis_size("gy") * bricks.shape[1]
    covariance = gram / total_cells
    factor = jnp.linalg.cholesky(covariance)
    for bit in range(lax.axis_size("gy").bit_length() - 1):
        other = from_partner(factor, "gy", bit)
        factor = combined(factor, other)
    for bit in range(lax.axis_size("gx").bit_length() - 1):
        other = from_partner(factor, "gx", bit)
        factor = combined(factor, other)
    kept = RANK
    modes = lax.linalg.triangular_solve(
        factor[:kept, :kept], bricks[:kept].astype(jnp.float32), left_side=True, lower=True
    )
    return (factor, modes)


def solution(mesh):
    in_specs = (
        P(None, ("gx", "gy")),
        P(("gx", "gy"), None),
        P(("gx", "gy")),
        P(("gx", "gy"), None),
        P(("gx", "gy"), None),
        P(),
    )
    out_specs = (P(), P(None, ("gx", "gy")))
    return jax.shard_map(body, mesh=mesh, in_specs=in_specs, out_specs=out_specs, check_vma=False)
```

profile of v0, /device:TPU:6, one launch (start us, length us, event | category | flops | bytes accessed | tf_op | source)
XLA Modules:
  0.0 605.3 jit_solution(3043925036575490538)
XLA Ops:
  17.1 11.6 %all-to-all-start = ((bf16[256,64,128]{2,0,1:T(8,128)(2,1)}), bf16[256,64,128]{2,0,1:T(8,128)(2,1)}, u32[]{:S(2)}, u32[]{:S(2)}) async-start(bf16[256,64,128]{2,0,1:T(8,128)(2,1)} %multiply_bitcast_fusion), calls=%async_computation | async-start | bytes 8388608 | tf_op jit(solution)/shard_map/all_to_all | solution.py:36
  37.2 22.5 %copy.81 = bf16[32,4,128,512]{2,3,1,0:T(8,128)(2,1)} copy(bf16[32,4,128,512]{3,2,1,0:T(8,128)(2,1)} %bitcast.181) | data formatting | bytes 33554432 | tf_op jit(solution)/shard_map/jit(_take)/gather | solution.py:18
  60.0 65.7 %all-to-all-done = bf16[256,64,128]{2,0,1:T(8,128)(2,1)} async-done(((bf16[256,64,128]{2,0,1:T(8,128)(2,1)}), bf16[256,64,128]{2,0,1:T(8,128)(2,1)}, u32[]{:S(2)}, u32[]{:S(2)}) %all-to-all-start) | async-done | bytes 4194336 | tf_op jit(solution)/shard_map/all_to_all | solution.py:36
  134.6 13.0 %fusion.3 = bf16[256,32,512]{0,2,1:T(8,128)(2,1)} fusion(bf16[32,4,256,128]{3,2,1,0:T(8,128)(2,1)} %bitcast.183, pred[32,4]{1,0:T(8,128)(4,1)S(1)} %copy.82, bf16[32,4,128,512]{2,3,1,0:T(8,128)(2,1)} %copy.81, pred[32,4]{1,0:T(8,128)(4,1)S(1)} %copy.79), kind=kOutput, calls=%fused_computation.7 | convolution fusion | flops 4311744512 | bytes 33554688 | tf_op jit(solution)/shard_map/sbnc,bncd->sbd/dot_general | solution.py:19
  157.0 11.7 %cholesky.424 = f32[128,128]{1,0:T(8,128)S(1)} custom-call(f32[128,128]{1,0:T(8,128)S(1)} %cholesky.726), custom_call_target="Cholesky" | custom-call | tf_op jit(solution)/shard_map/jit(cholesky)/cholesky | solution.py:43
  179.0 12.1 %cholesky.441 = f32[128,128]{1,0:T(8,128)S(1)} custom-call(f32[128,128]{1,0:T(8,128)S(1)} %convolution_subtract_fusion), custom_call_target="Cholesky" | custom-call | tf_op jit(solution)/shard_map/jit(cholesky)/cholesky | solution.py:43
  202.0 11.7 %cholesky.458 = f32[128,128]{1,0:T(8,128)S(1)} custom-call(f32[128,128]{1,0:T(8,128)S(1)} %cholesky.729), custom_call_target="Cholesky" | custom-call | tf_op jit(solution)/shard_map/jit(cholesky)/cholesky | solution.py:26
  225.4 11.7 %cholesky.475 = f32[128,128]{1,0:T(8,128)S(1)} custom-call(f32[128,128]{1,0:T(8,128)S(1)} %slice_subtract_fusion.7), custom_call_target="Cholesky" | custom-call | tf_op jit(solution)/shard_map/jit(cholesky)/cholesky | solution.py:26
  242.8 11.9 %collective-permute-done.1 = f32[256,256]{1,0:T(8,128)S(1)} collective-permute-done((f32[256,256]{1,0:T(8,128)S(1)}, f32[256,256]{1,0:T(8,128)S(1)}, u32[]{:S(2)}, u32[]{:S(2)}) %collective-permute-start.1) | collective-permute-done | bytes 262176 | tf_op jit(solution)/shard_map/ppermute | solution.py:13
  255.3 11.7 %cholesky.492 = f32[128,128]{1,0:T(8,128)S(1)} custom-call(f32[128,128]{1,0:T(8,128)S(1)} %cholesky.732), custom_call_target="Cholesky" | custom-call | tf_op jit(solution)/shard_map/jit(cholesky)/cholesky | solution.py:26
  278.7 11.7 %cholesky.509 = f32[128,128]{1,0:T(8,128)S(1)} custom-call(f32[128,128]{1,0:T(8,128)S(1)} %slice_subtract_fusion.6), custom_call_target="Cholesky" | custom-call | tf_op jit(solution)/shard_map/jit(cholesky)/cholesky | solution.py:26
  298.9 11.9 %collective-permute-done.2 = f32[256,256]{1,0:T(8,128)S(1)} collective-permute-done((f32[256,256]{1,0:T(8,128)S(1)}, f32[256,256]{1,0:T(8,128)S(1)}, u32[]{:S(2)}, u32[]{:S(2)}) %collective-permute-start.2) | collective-permute-done | bytes 262176 | tf_op jit(solution)/shard_map/ppermute | solution.py:13
  311.5 11.7 %cholesky.526 = f32[128,128]{1,0:T(8,128)S(1)} custom-call(f32[128,128]{1,0:T(8,128)S(1)} %cholesky.735), custom_call_target="Cholesky" | custom-call | tf_op jit(solution)/shard_map/jit(cholesky)/cholesky | solution.py:26
  334.9 11.7 %cholesky.543 = f32[128,128]{1,0:T(8,128)S(1)} custom-call(f32[128,128]{1,0:T(8,128)S(1)} %slice_subtract_fusion.5), custom_call_target="Cholesky" | custom-call | tf_op jit(solution)/shard_map/jit(cholesky)/cholesky | solution.py:26
  360.5 11.7 %cholesky.560 = f32[128,128]{1,0:T(8,128)S(1)} custom-call(f32[128,128]{1,0:T(8,128)S(1)} %cholesky.738), custom_call_target="Cholesky" | custom-call | tf_op jit(solution)/shard_map/jit(cholesky)/cholesky | solution.py:26
  383.9 11.7 %cholesky.577 = f32[128,128]{1,0:T(8,128)S(1)} custom-call(f32[128,128]{1,0:T(8,128)S(1)} %slice_subtract_fusion.4), custom_call_target="Cholesky" | custom-call | tf_op jit(solution)/shard_map/jit(cholesky)/cholesky | solution.py:26
  409.6 11.7 %cholesky.594 = f32[128,128]{1,0:T(8,128)S(1)} custom-call(f32[128,128]{1,0:T(8,128)S(1)} %cholesky.741), custom_call_target="Cholesky" | custom-call | tf_op jit(solution)/shard_map/jit(cholesky)/cholesky | solution.py:26
  432.9 11.7 %cholesky.611 = f32[128,128]{1,0:T(8,128)S(1)} custom-call(f32[128,128]{1,0:T(8,128)S(1)} %slice_subtract_fusion.3), custom_call_target="Cholesky" | custom-call | tf_op jit(solution)/shard_map/jit(cholesky)/cholesky | solution.py:26
  451.4 11.7 %cholesky.628 = f32[128,128]{1,0:T(8,128)S(1)} custom-call(f32[128,128]{1,0:T(8,128)S(1)} %cholesky.744), custom_call_target="Cholesky" | custom-call | tf_op jit(solution)/shard_map/jit(cholesky)/cholesky | solution.py:26
  474.8 11.7 %cholesky.645 = f32[128,128]{1,0:T(8,128)S(1)} custom-call(f32[128,128]{1,0:T(8,128)S(1)} %slice_subtract_fusion.2), custom_call_target="Cholesky" | custom-call | tf_op jit(solution)/shard_map/jit(cholesky)/cholesky | solution.py:26
  500.3 11.7 %cholesky.662 = f32[128,128]{1,0:T(8,128)S(1)} custom-call(f32[128,128]{1,0:T(8,128)S(1)} %cholesky.747), custom_call_target="Cholesky" | custom-call | tf_op jit(solution)/shard_map/jit(cholesky)/cholesky | solution.py:26
  523.7 11.7 %cholesky.679 = f32[128,128]{1,0:T(8,128)S(1)} custom-call(f32[128,128]{1,0:T(8,128)S(1)} %slice_subtract_fusion.1), custom_call_target="Cholesky" | custom-call | tf_op jit(solution)/shard_map/jit(cholesky)/cholesky | solution.py:26
  549.6 11.7 %cholesky.696 = f32[128,128]{1,0:T(8,128)S(1)} custom-call(f32[128,128]{1,0:T(8,128)S(1)} %cholesky.750), custom_call_target="Cholesky" | custom-call | tf_op jit(solution)/shard_map/jit(cholesky)/cholesky | solution.py:26
  571.7 11.7 %cholesky.713 = f32[128,128]{1,0:T(8,128)S(1)} custom-call(f32[128,128]{1,0:T(8,128)S(1)} %slice_subtract_fusion), custom_call_target="Cholesky" | custom-call | tf_op jit(solution)/shard_map/jit(cholesky)/cholesky | solution.py:26
  (181 shorter events, 243.9 us)
Async XLA Ops:
  0.6 28.5 %copy-start = (bf16[4,128,512]{2,1,0:T(8,128)(2,1)S(1)}, bf16[4,128,512]{2,1,0:T(8,128)(2,1)}, u32[]{:S(2)}) copy-start(bf16[4,128,512]{2,1,0:T(8,128)(2,1)} %param.12) | copy-start | bytes 1572868
  0.6 8.4 %copy-start.6 = (s32[32]{0:T(128)S(1)}, s32[32]{0:T(128)}, u32[]{:S(2)}) copy-start(s32[32]{0:T(128)} %param.9) | copy-start | bytes 388
  12.3 16.3 %copy-start.4 = (s32[32,4]{0,1:T(4,128)S(1)}, s32[32,4]{0,1:T(4,128)}, u32[]{:S(2)}) copy-start(s32[32,4]{0,1:T(4,128)} %param.10) | copy-start | bytes 1540
  12.3 16.4 %copy-start.5 = (s32[32,4]{0,1:T(4,128)S(1)}, s32[32,4]{0,1:T(4,128)}, u32[]{:S(2)}) copy-start(s32[32,4]{0,1:T(4,128)} %param.11) | copy-start | bytes 1540
  17.1 108.6 %all-to-all-start = ((bf16[256,64,128]{2,0,1:T(8,128)(2,1)}), bf16[256,64,128]{2,0,1:T(8,128)(2,1)}, u32[]{:S(2)}, u32[]{:S(2)}) async-start(bf16[256,64,128]{2,0,1:T(8,128)(2,1)} %multiply_bitcast_fusion), calls=%async_computation | async-start | bytes 8388608 | tf_op jit(solution)/shard_map/all_to_all | solution.py:36
  191.2 2.7 copy-start.2
  194.9 6.5 %collective-permute-start = (f32[256,256]{1,0:T(8,128)S(1)}, f32[256,256]{1,0:T(8,128)S(1)}, u32[]{:S(2)}, u32[]{:S(2)}) collective-permute-start(f32[256,256]{1,0:T(8,128)S(1)} %fusion.23), channel_id=1, source_target_pairs={{0,1},{1,0},{2,3},{3,2},{4,5},{5,4},{6,7},{7,6},{8,9},{9,8},{10,11... | collective-permute-start | bytes 786440 | tf_op jit(solution)/shard_map/ppermute | solution.py:13
  241.4 13.2 %collective-permute-start.1 = (f32[256,256]{1,0:T(8,128)S(1)}, f32[256,256]{1,0:T(8,128)S(1)}, u32[]{:S(2)}, u32[]{:S(2)}) collective-permute-start(f32[256,256]{1,0:T(8,128)S(1)} %fusion.24), channel_id=1, source_target_pairs={{0,2},{1,3},{2,0},{3,1},{4,6},{5,7},{6,4},{7,5},{8,10},{9,11},{10,... | collective-permute-start | bytes 786440 | tf_op jit(solution)/shard_map/ppermute | solution.py:13
  294.7 16.2 %collective-permute-start.2 = (f32[256,256]{1,0:T(8,128)S(1)}, f32[256,256]{1,0:T(8,128)S(1)}, u32[]{:S(2)}, u32[]{:S(2)}) collective-permute-start(f32[256,256]{1,0:T(8,128)S(1)} %fusion.25), channel_id=1, source_target_pairs={{0,4},{1,5},{2,6},{3,7},{4,0},{5,1},{6,2},{7,3},{8,12},{9,13},{10,... | collective-permute-start | bytes 786440 | tf_op jit(solution)/shard_map/ppermute | solution.py:13
  350.9 9.0 %collective-permute-start.3 = (f32[256,256]{1,0:T(8,128)S(1)}, f32[256,256]{1,0:T(8,128)S(1)}, u32[]{:S(2)}, u32[]{:S(2)}) collective-permute-start(f32[256,256]{1,0:T(8,128)S(1)} %fusion.26), channel_id=1, source_target_pairs={{0,8},{1,9},{2,10},{3,11},{4,12},{5,13},{6,14},{7,15},{8,0},{9,1},... | collective-permute-start | bytes 786440 | tf_op jit(solution)/shard_map/ppermute | solution.py:13
  399.9 9.0 %collective-permute-start.4 = (f32[256,256]{1,0:T(8,128)S(1)}, f32[256,256]{1,0:T(8,128)S(1)}, u32[]{:S(2)}, u32[]{:S(2)}) collective-permute-start(f32[256,256]{1,0:T(8,128)S(1)} %fusion.27), channel_id=1, source_target_pairs={{0,16},{1,17},{2,18},{3,19},{4,20},{5,21},{6,22},{7,23},{8,24},{9,... | collective-permute-start | bytes 786440 | tf_op jit(solution)/shard_map/ppermute | solution.py:13
  449.0 1.8 collective-permute-start.5
  490.9 8.8 %collective-permute-start.6 = (f32[256,256]{1,0:T(8,128)S(1)}, f32[256,256]{1,0:T(8,128)S(1)}, u32[]{:S(2)}, u32[]{:S(2)}) collective-permute-start(f32[256,256]{1,0:T(8,128)S(1)} %fusion.29), channel_id=1, source_target_pairs={{0,64},{32,96},{64,0},{96,32},{128,192},{160,224},{192,128},{224,1... | collective-permute-start | bytes 786440 | tf_op jit(solution)/shard_map/ppermute | solution.py:13
  539.7 9.2 %collective-permute-start.7 = (f32[256,256]{1,0:T(8,128)S(1)}, f32[256,256]{1,0:T(8,128)S(1)}, u32[]{:S(2)}, u32[]{:S(2)}) collective-permute-start(f32[256,256]{1,0:T(8,128)S(1)} %fusion.30), channel_id=1, source_target_pairs={{0,128},{32,160},{64,192},{96,224},{128,0},{160,32},{192,64},{224,... | collective-permute-start | bytes 786440 | tf_op jit(solution)/shard_map/ppermute | solution.py:13
  545.9 59.3 %copy-start.1 = (bf16[4,128,512]{2,1,0:T(8,128)(2,1)S(1)}, bf16[4,128,512]{2,1,0:T(8,128)(2,1)}, u32[]{:S(2)}) copy-start(bf16[4,128,512]{2,1,0:T(8,128)(2,1)} %param.12) | copy-start | bytes 1572868
  586.0 19.1 %copy-start.3 = (f32[256,256]{1,0:T(8,128)}, f32[256,256]{1,0:T(8,128)S(1)}, u32[]{:S(2)}) copy-start(f32[256,256]{1,0:T(8,128)S(1)} %select_select_fusion) | copy-start | bytes 786436
where the time goes:
time: 612 us; the launch traced here: 605 us
  other arithmetic  339 us (55%)
  waiting for transfers between devices  118 us (19%)
  local copies, waits for them, and re-layouts  62.6 us (10%)
  matrix products  46.5 us (8%)
  starting transfers between devices  25.5 us (4%)
  between operations  13.6 us (2%)
    another operation x56, other arithmetic, combined(): return jnp.linalg.cholesky(mine + theirs)  281 us
    all_to_all x1, waiting for transfers between devices, body(): lax.all_to_all(outgoing, 'gy', split_axis=1, concat_axis=1, tiled=True)  65.7 us
    ppermute x8, waiting for transfers between devices, from_partner(): return lax.ppermute(value, axis, pairs)  52.1 us
    another operation x7, other arithmetic, body(): factor = jnp.linalg.cholesky(covariance)  35 us
    gather x2, local copies, waits for them, and re-layouts, lift(): chosen = jnp.take(maps, levels, axis=0)  30.6 us
    ppermute x8, starting transfers between devices, from_partner(): return lax.ppermute(value, axis, pairs)  13.8 us
    dot_general x1, matrix products, lift(): jnp.einsum('sbnc,bncd->sbd', picked, chosen, preferred_element_type=jnp.f...  13 us
  transfers between devices with their start and end apart: 9, of which 9 were waited for; matrix products, arithmetic and copies ran while one was open for 6% of the time, Pallas kernels for 0%

commit v1 on v0

--- a/solution.py
+++ b/solution.py
@@ -39,14 +39,9 @@
         bricks, bricks, (((1,), (1,)), ((), ())), preferred_element_type=jnp.float32
     )
     total_cells = lax.axis_size("gx") * lax.axis_size("gy") * bricks.shape[1]
+    gram = lax.psum(gram, ("gx", "gy"))
     covariance = gram / total_cells
     factor = jnp.linalg.cholesky(covariance)
-    for bit in range(lax.axis_size("gy").bit_length() - 1):
-        other = from_partner(factor, "gy", bit)
-        factor = combined(factor, other)
-    for bit in range(lax.axis_size("gx").bit_length() - 1):
-        other = from_partner(factor, "gx", bit)
-        factor = combined(factor, other)
     kept = RANK
     modes = lax.linalg.triangular_solve(
         factor[:kept, :kept], bricks[:kept].astype(jnp.float32), left_side=True, lower=True

time: 612 us -> 480 us (0.78)
  other arithmetic: 339 us -> 50.8 us
  waiting for transfers between devices: 118 us -> 312 us
  matrix products: 46.5 us -> 32.2 us
  starting transfers between devices: 25.5 us -> 11.7 us
    another operation x56 -> x0, other arithmetic: 281 us -> none  [combined(): return jnp.linalg.cholesky(mine + theirs)]
    psum x0 -> x1, waiting for transfers between devices: none -> 246 us  [body(): gram = lax.psum(gram, ('gx', 'gy'))]
    ppermute x8 -> x0, waiting for transfers between devices: 52.1 us -> none  [from_partner(): return lax.ppermute(value, axis, pairs)]
    ppermute x8 -> x0, starting transfers between devices: 13.8 us -> none  [from_partner(): return lax.ppermute(value, axis, pairs)]
    another operation x16 -> x0, matrix products: 8.21 us -> none  [combined(): return jnp.linalg.cholesky(mine + theirs)]
    select_n x8 -> x1, other arithmetic: 6.89 us -> 0.01 us  [lift(): chosen = jnp.take(maps, levels, axis=0)]
    dot_general x16 -> x0, matrix products: 6.58 us -> none  [the longest x8 3.31 us: combined(): theirs = jnp.dot(other, other.T, precision=lax.Precision.HIGHEST)]
    another operation x7 -> x6, other arithmetic: 35 us -> 34.2 us  [body(): factor = jnp.linalg.cholesky(covariance)]
  transfers between devices with their start and end apart: 9 -> 2, of which waited for: 9 -> 2; matrix products, arithmetic and copies ran while one was open for 6% -> 8% of each run, Pallas kernels for 0% -> 0%
where the time goes in v1:
time: 480 us; the launch traced here: 479 us
  waiting for transfers between devices  312 us (65%)
  local copies, waits for them, and re-layouts  56.6 us (12%)
  other arithmetic  50.8 us (11%)
  matrix products  32.2 us (7%)
  between operations  15.5 us (3%)
  starting transfers between devices  11.7 us (2%)
    psum x1, waiting for transfers between devices, body(): gram = lax.psum(gram, ('gx', 'gy'))  246 us
    all_to_all x1, waiting for transfers between devices, body(): lax.all_to_all(outgoing, 'gy', split_axis=1, concat_axis=1, tiled=True)  65.5 us
    another operation x6, other arithmetic, body(): factor = jnp.linalg.cholesky(covariance)  34.2 us
    gather x2, local copies, waits for them, and re-layouts, lift(): chosen = jnp.take(maps, levels, axis=0)  30.7 us
    dot_general x1, matrix products, lift(): jnp.einsum('sbnc,bncd->sbd', picked, chosen, preferred_element_type=jnp.f...  12.8 us
    all_to_all x1, starting transfers between devices, body(): lax.all_to_all(outgoing, 'gy', split_axis=1, concat_axis=1, tiled=True)  11.6 us
    dot_general x1, matrix products, body(): lax.dot_general(bricks, bricks, (((1,), (1,)), ((), ())), preferred_eleme...  9.83 us
    another operation x2, other arithmetic, body(): lax.linalg.triangular_solve(factor[:kept, :kept], bricks[:kept].astype(jn...  9.82 us
  transfers between devices with their start and end apart: 2, of which 2 were waited for; matrix products, arithmetic and copies ran while one was open for 8% of the time, Pallas kernels for 0%

profile of v1, /device:TPU:6, one launch (start us, length us, event | category | flops | bytes accessed | tf_op | source)
XLA Modules:
  0.0 478.6 jit_solution(10285981647548982762)
XLA Ops:
  7.2 0.8 copy.35
  8.3 4.1 copy.36
  12.3 3.2 copy.38
  15.8 3.1 gather_fusion.1
  18.9 4.7 multiply_bitcast_fusion
  23.6 11.6 %all-to-all-start = ((bf16[256,64,128]{2,0,1:T(8,128)(2,1)}), bf16[256,64,128]{2,0,1:T(8,128)(2,1)}, u32[]{:S(2)}, u32[]{:S(2)}) async-start(bf16[256,64,128]{2,0,1:T(8,128)(2,1)} %multiply_bitcast_fusion), calls=%async_computation | async-start | bytes 8388608 | tf_op jit(solution)/shard_map/all_to_all | solution.py:36
  35.7 8.1 %gather_fusion = bf16[128,128,512]{2,1,0:T(8,128)(2,1)} fusion(bf16[4,128,512]{2,1,0:T(8,128)(2,1)S(1)} %copy-done, s32[1024]{0:T(1024)S(1)} %pad_clamp_fusion.2), kind=kCustom, calls=%fused_computation | custom fusion | bytes 33554944 | tf_op jit(solution)/shard_map/jit(_take)/gather | solution.py:18
  43.9 22.6 %copy.33 = bf16[32,4,128,512]{2,3,1,0:T(8,128)(2,1)} copy(bf16[32,4,128,512]{3,2,1,0:T(8,128)(2,1)} %bitcast.43) | data formatting | bytes 33554432 | tf_op jit(solution)/shard_map/jit(_take)/gather | solution.py:18
  66.7 65.5 %all-to-all-done = bf16[256,64,128]{2,0,1:T(8,128)(2,1)} async-done(((bf16[256,64,128]{2,0,1:T(8,128)(2,1)}), bf16[256,64,128]{2,0,1:T(8,128)(2,1)}, u32[]{:S(2)}, u32[]{:S(2)}) %all-to-all-start) | async-done | bytes 4194336 | tf_op jit(solution)/shard_map/all_to_all | solution.py:36
  132.2 8.9 %gather_fusion.2 = bf16[128,256,128]{2,1,0:T(8,128)(2,1)} fusion(bf16[256,64,128]{2,0,1:T(8,128)(2,1)} %all-to-all-done, s32[1024]{0:T(1024)S(1)} %pad_clamp_fusion), kind=kCustom, calls=%fused_computation.2 | custom fusion | bytes 16777728 | tf_op jit(solution)/shard_map/jit(_take)/gather | solution.py:17
  141.1 12.8 %fusion.3 = bf16[256,32,512]{0,2,1:T(8,128)(2,1)} fusion(bf16[32,4,256,128]{3,2,1,0:T(8,128)(2,1)} %bitcast.45, pred[32,4]{1,0:T(8,128)(4,1)S(1)} %copy.34, bf16[32,4,128,512]{2,3,1,0:T(8,128)(2,1)} %copy.33, pred[32,4]{1,0:T(8,128)(4,1)S(1)} %copy.31), kind=kOutput, calls=%fused_computation.7 | convolution fusion | flops 4311744512 | bytes 33554688 | tf_op jit(solution)/shard_map/sbnc,bncd->sbd/dot_general | solution.py:19
  154.0 9.8 %convolution_bitcast_fusion = f32[256,256]{0,1:T(8,128)} fusion(bf16[256,32,512]{0,2,1:T(8,128)(2,1)} %fusion.3), kind=kOutput, calls=%fused_computation.14 | convolution fusion | flops 2147483648 | bytes 8650752 | tf_op jit(solution)/shard_map/dot_general | solution.py:38
  163.8 4.6 triangular_solve.20
  168.5 246.3 %all-reduce.3.cloned.1.call-done = f32[256,256]{0,1:T(8,128)} async-done(((f32[256,256]{0,1:T(8,128)}), f32[256,256]{0,1:T(8,128)}) %all-reduce.3.cloned.1.call-update) | async-done | bytes 262160 | tf_op jit(solution)/shard_map/psum | solution.py:42
  414.7 1.0 broadcast_multiply_fusion
  415.9 1.0 fusion.13
  416.9 11.7 %cholesky.53 = f32[128,128]{1,0:T(8,128)S(1)} custom-call(f32[128,128]{1,0:T(8,128)S(1)} %cholesky.124), custom_call_target="Cholesky" | custom-call | tf_op jit(solution)/shard_map/jit(cholesky)/cholesky | solution.py:44
  428.6 9.8 %custom-call.14 = f32[1,128,128]{1,2,0:T(8,128)S(1)} custom-call(f32[1,128,128]{2,1,0:T(8,128)S(1)} %get-tuple-element.5), custom_call_target="InvertDiagBlocksLowerTriangular" | custom-call | tf_op jit(solution)/shard_map/jit(cholesky)/cholesky | solution.py:44
  438.5 0.2 constant_dynamic-update-slice_fusion.1
  438.7 0.3 convolution_subtract_fusion
  438.9 11.9 %cholesky.111 = f32[128,128]{1,0:T(8,128)S(1)} custom-call(f32[128,128]{1,0:T(8,128)S(1)} %convolution_subtract_fusion), custom_call_target="Cholesky" | custom-call | tf_op jit(solution)/shard_map/jit(cholesky)/cholesky | solution.py:44
  450.9 0.6 compare_reduce_fusion
  452.9 9.8 %custom-call.15 = f32[1,128,128]{1,2,0:T(8,128)S(1)} custom-call(f32[1,128,128]{2,1,0:T(8,128)S(1)} %fusion.14), custom_call_target="InvertDiagBlocksLowerTriangular" | custom-call | tf_op jit(solution)/shard_map/triangular_solve | solution.py:46
  462.7 9.1 %fusion.17 = f32[128,16384]{1,0:T(8,128)} fusion(bf16[128,16384]{0,1:T(8,128)(2,1)} %bitcast.44, f32[1,128,128]{1,2,0:T(8,128)S(1)} %custom-call.15), kind=kOutput, calls=%fused_computation.25 | convolution fusion | flops 3221225472 | bytes 12648448 | tf_op jit(solution)/shard_map/triangular_solve | solution.py:46
  (40 shorter events, 1.4 us)
Async XLA Ops:
  7.2 28.5 %copy-start = (bf16[4,128,512]{2,1,0:T(8,128)(2,1)S(1)}, bf16[4,128,512]{2,1,0:T(8,128)(2,1)}, u32[]{:S(2)}) copy-start(bf16[4,128,512]{2,1,0:T(8,128)(2,1)} %param.11) | copy-start | bytes 1572868
  7.2 8.4 %copy-start.5 = (s32[32]{0:T(128)S(1)}, s32[32]{0:T(128)}, u32[]{:S(2)}) copy-start(s32[32]{0:T(128)} %param.8) | copy-start | bytes 388
  18.9 16.4 %copy-start.4 = (s32[32,4]{0,1:T(4,128)S(1)}, s32[32,4]{0,1:T(4,128)}, u32[]{:S(2)}) copy-start(s32[32,4]{0,1:T(4,128)} %param.9) | copy-start | bytes 1540
  18.9 16.6 %copy-start.3 = (s32[32,4]{0,1:T(4,128)S(1)}, s32[32,4]{0,1:T(4,128)}, u32[]{:S(2)}) copy-start(s32[32,4]{0,1:T(4,128)} %param.10) | copy-start | bytes 1540
  23.6 108.6 %all-to-all-start = ((bf16[256,64,128]{2,0,1:T(8,128)(2,1)}), bf16[256,64,128]{2,0,1:T(8,128)(2,1)}, u32[]{:S(2)}, u32[]{:S(2)}) async-start(bf16[256,64,128]{2,0,1:T(8,128)(2,1)} %multiply_bitcast_fusion), calls=%async_computation | async-start | bytes 8388608 | tf_op jit(solution)/shard_map/all_to_all | solution.py:36
  35.2 379.5 %all-reduce.3.cloned.1.call-start = ((), (), s32[]{:S(2)}) async-start(), calls=%async_computation.1 | async-start | bytes 524288 | tf_op jit(solution)/shard_map/psum | solution.py:42
  163.8 307.9 %copy-start.1 = (bf16[4,128,512]{2,1,0:T(8,128)(2,1)S(1)}, bf16[4,128,512]{2,1,0:T(8,128)(2,1)}, u32[]{:S(2)}) copy-start(bf16[4,128,512]{2,1,0:T(8,128)(2,1)} %param.11) | copy-start | bytes 1572868
  452.9 18.9 %copy-start.2 = (f32[256,256]{1,0:T(8,128)}, f32[256,256]{1,0:T(8,128)S(1)}, u32[]{:S(2)}) copy-start(f32[256,256]{1,0:T(8,128)S(1)} %select_select_fusion) | copy-start | bytes 786436
Sparse Core Ops, SparseCore 0:
  163.9 250.7 all-reduce.2
